TPU v7x, 128 devices: a whole 4x4x4 slice. The times are simulated.
128 devices in a mesh: row: 8 (over z_hi, x), col: 16 (over z_lo, y, core).
Axes of the slice: x: 4, y: 4, z: 4 (z_hi: 2, z_lo: 2; z = z_hi * 2 + z_lo), core: 2. Of those that a mesh axis runs over, the one named last changes fastest.
Arguments:
- tokens: bfloat16 [1024, 8192], P(('row', 'col')), may hold values from -6 to 6
- gain: float32 [8192], replicated, may hold values from 0.5 to 1.5
- grad_out: bfloat16 [1024, 8192], P(('row', 'col')), may hold values from -4 to 4
- pre_gate: bfloat16 [1024, 28672], P('col', 'row'), may hold values from -6 to 6
- pre_up: bfloat16 [1024, 28672], P('col', 'row'), may hold values from -6 to 6
- gate_weight: bfloat16 [8192, 28672], P('col', 'row'), may hold values from -0.0625 to 0.0625
- up_weight: bfloat16 [8192, 28672], P('col', 'row'), may hold values from -0.0625 to 0.0625
- down_weight: bfloat16 [28672, 8192], P('row', 'col'), may hold values from -0.03125 to 0.03125
Outputs:
- grad_tokens: bfloat16 [1024, 8192], P(('row', 'col'))
- grad_gain: float32 [8192], replicated
- grad_gate: bfloat16 [8192, 28672], P('col', 'row')
- grad_up: bfloat16 [8192, 28672], P('col', 'row')
- grad_down: bfloat16 [28672, 8192], P('row', 'col')
All inputs are finite; a program needn't handle non-finite values.
Results may differ from a plain program's by a relative error of at most 0.0057.
Values may be sent and summed in bfloat16 or wider, within the bound.
No kernel may reach another device: no remote copies, remote signals or barrier semaphores. Data moves between devices by JAX's collectives and lax.ppermute only.
A program may use at most 192 MiB of HBM per device.

v0:
```python
import jax
import jax.numpy as jnp
from jax import lax
from jax.sharding import PartitionSpec as P

epsilon = 1e-05


def swiglu_grads(hidden_grad, pre_gate, pre_up):
    gate_wide = pre_gate.astype(jnp.float32)
    up_wide = pre_up.astype(jnp.float32)
    sigmoid = jax.nn.sigmoid(gate_wide)
    silu = gate_wide * sigmoid
    hidden = (silu * up_wide).astype(jnp.bfloat16)
    up_grad = (hidden_grad * silu).astype(jnp.bfloat16)
    gate_grad = (hidden_grad * up_wide * sigmoid * (1.0 + gate_wide * (1.0 - sigmoid))).astype(
        jnp.bfloat16
    )
    return (hidden, gate_grad, up_grad)


def row_gather(x):
    rows = lax.axis_size("row")
    copies = jnp.broadcast_to(x[None], (rows,) + x.shape)
    got = lax.all_to_all(copies, "row", split_axis=0, concat_axis=0, tiled=True)
    return got.reshape((rows * x.shape[0],) + x.shape[1:])


def local(tokens, gain, grad_out, pre_gate, pre_up, gate_weight, up_weight, down_weight):
    cols = lax.axis_size("col")
    rows = lax.axis_size("row")
    tokens_wide = tokens.astype(jnp.float32)
    inverse_rms = lax.rsqrt(jnp.mean(tokens_wide * tokens_wide, axis=1, keepdims=True) + epsilon)
    normed = tokens_wide * inverse_rms
    tile = gate_weight.shape[0]
    gain_tile = lax.dynamic_slice_in_dim(gain, lax.axis_index("col") * tile, tile)
    mine_rows = tokens.shape[0]
    lanes = 128
    grid_grad = lax.all_to_all(grad_out, "col", split_axis=1, concat_axis=0, tiled=True)
    packed = jnp.concatenate(
        [
            tokens_wide.reshape(mine_rows, cols, tile),
            jnp.broadcast_to(inverse_rms[:, :, None], (mine_rows, cols, lanes)),
        ],
        axis=2,
    )
    grid = lax.all_to_all(packed, "col", split_axis=1, concat_axis=0, tiled=True)
    grid = grid.reshape(cols * mine_rows, tile + lanes)
    grid_tokens = grid[:, :tile].astype(jnp.bfloat16)
    grid_scale = grid[:, tile : tile + 1].reshape(1, cols * mine_rows)
    all_grad = row_gather(grid_grad)
    hidden_block = swiglu_grads(jnp.zeros(pre_gate.shape, jnp.float32), pre_gate, pre_up)[0]
    split = hidden_block.shape[1] // 448 * 128
    hidden_piece = lax.all_gather(hidden_block[:, :split], "col", axis=0, tiled=True)
    partial_grad = jnp.einsum(
        "td,fd->tf", all_grad, down_weight, preferred_element_type=jnp.float32
    )
    hidden_piece, partial_grad = lax.optimization_barrier((hidden_piece, partial_grad))
    block_grad = lax.psum_scatter(partial_grad, "col", scatter_dimension=0, tiled=True)
    down_total = jnp.einsum("tf,td->fd", hidden_piece, all_grad, preferred_element_type=jnp.float32)
    down_total, block_grad = lax.optimization_barrier((down_total, block_grad))
    _, gate_block, up_block = swiglu_grads(block_grad, pre_gate, pre_up)
    all_tokens = row_gather(grid_tokens).astype(jnp.float32)
    all_scale = row_gather(grid_scale).reshape(-1, 1)
    all_normed = all_tokens * all_scale
    all_input = (all_normed * gain_tile).astype(jnp.bfloat16)
    gate_piece = lax.all_gather(gate_block, "col", axis=0, tiled=True)
    up_piece = lax.all_gather(up_block, "col", axis=0, tiled=True)
    gate_total = jnp.einsum("td,tf->df", all_input, gate_piece, preferred_element_type=jnp.float32)
    gate_total, up_piece = lax.optimization_barrier((gate_total, up_piece))
    late_block, up_piece = lax.optimization_barrier((hidden_block[:, split:], up_piece))
    late_piece = lax.all_gather(late_block, "col", axis=0, tiled=True)
    new_rows = jnp.einsum("tf,df->td", gate_piece, gate_weight, preferred_element_type=jnp.float32)
    new_rows = new_rows + jnp.einsum(
        "tf,df->td", up_piece, up_weight, preferred_element_type=jnp.float32
    )
    gain_part = jnp.sum(new_rows * all_normed, axis=0)
    tokens_all = new_rows.shape[0]
    blocks = new_rows.astype(jnp.bfloat16).reshape(rows, tokens_all // rows, tile)
    gain_high = gain_part.astype(jnp.bfloat16)
    gain_low = (gain_part - gain_high.astype(jnp.float32)).astype(jnp.bfloat16)
    extra = jnp.zeros((rows, 8, tile), jnp.bfloat16)
    extra = extra.at[:, 0, :].set(gain_high).at[:, 1, :].set(gain_low)
    sent = jnp.concatenate([blocks, extra], axis=1)
    got = lax.all_to_all(sent, "row", split_axis=0, concat_axis=0, tiled=True)
    summed = jnp.sum(got.astype(jnp.float32), axis=0)
    grid_back = summed[: tokens_all // rows]
    gain_tile_grad = summed[tokens_all // rows] + summed[tokens_all // rows + 1]
    per_col = grid_back.reshape(cols, -1, tile)
    mine = per_col.shape[1]
    sent2 = jnp.concatenate(
        [per_col, jnp.broadcast_to(gain_tile_grad[None, None, :], (cols, 1, tile))], axis=1
    )
    got2 = lax.all_to_all(sent2, "col", split_axis=0, concat_axis=0, tiled=True)
    normed_grad = got2[:, :mine, :].transpose(1, 0, 2).reshape(mine, cols * tile)
    grad_gain = got2[:, mine, :].reshape(cols * tile)
    up_total = jnp.einsum("td,tf->df", all_input, up_piece, preferred_element_type=jnp.float32)
    down_late = jnp.einsum("tf,td->fd", late_piece, all_grad, preferred_element_type=jnp.float32)
    scaled_grad = normed_grad * gain
    inner = jnp.mean(scaled_grad * normed, axis=1, keepdims=True)
    grad_tokens = (
        grad_out.astype(jnp.float32) + inverse_rms * (scaled_grad - normed * inner)
    ).astype(jnp.bfloat16)
    return (
        grad_tokens,
        grad_gain,
        gate_total.astype(jnp.bfloat16),
        up_total.astype(jnp.bfloat16),
        jnp.concatenate([down_total, down_late], axis=0).astype(jnp.bfloat16),
    )


def solution(mesh):
    in_specs = (
        P(("row", "col"), None),
        P(),
        P(("row", "col"), None),
        P("col", "row"),
        P("col", "row"),
        P("col", "row"),
        P("col", "row"),
        P("row", "col"),
    )
    out_specs = (P(("row", "col"), None), P(), P("col", "row"), P("col", "row"), P("row", "col"))
    return jax.shard_map(local, mesh=mesh, in_specs=in_specs, out_specs=out_specs, check_vma=False)
```

profile of v0, /device:TPU:1, one launch (start us, length us, event | category | flops | bytes accessed | tf_op | source)
XLA Modules:
  0.0 330.3 jit_solution(11313620677822065228)
XLA Ops:
  7.2 1.4 fusion.4
  8.6 0.7 slice.76
  9.4 13.4 %all_to_all.56 = bf16[8,16,512]{2,0,1:T(8,128)(2,1)S(1)} all-to-all(bf16[8,16,512]{2,0,1:T(8,128)(2,1)} %bitcast.49), channel_id=1, replica_groups=mesh['row'=8,'col'=16] {'col'}, dimensions={1} | all-to-all | bytes 262144 | tf_op jit(solution)/shard_map/all_to_all | solution.py:39
  22.9 23.5 %all_to_all.57 = bf16[8,128,512]{2,1,0:T(8,128)(2,1)S(1)} all-to-all(bf16[8,128,512]{2,1,0:T(8,128)(2,1)S(1)} %broadcast_in_dim.15), channel_id=1, replica_groups=mesh['row'=8,'col'=16] {'row'}, dimensions={0} | all-to-all | bytes 2097152 | tf_op jit(solution)/shard_map/all_to_all | solution.py:25
  46.4 1.0 copy-done.4
  47.4 9.4 %fusion.13 = f32[1024,3584]{1,0:T(8,128)} fusion(bf16[1024,512]{1,0:T(8,128)(2,1)S(1)} %bitcast.42, bf16[3584,512]{1,0:T(8,128)(2,1)} %param.19), kind=kOutput, calls=%fused_computation.38 | convolution fusion | flops 3758096384 | bytes 19398656 | tf_op jit(solution)/shard_map/td,fd->tf/dot_general | solution.py:55
  56.9 3.2 fusion.14
  60.1 84.9 %reduce-scatter.2.cloned.1.call-done = f32[64,3584]{1,0:T(8,128)} async-done(((f32[1024,3584]{1,0:T(8,128)}), f32[64,3584]{1,0:T(8,128)}) %reduce-scatter.2.cloned.1.call-update) | async-done | bytes 917520 | tf_op jit(solution)/shard_map/reduce_scatter | solution.py:59
  145.0 2.5 multiply_convert_fusion
  148.5 14.1 %all_to_all.58 = f32[8,16,640]{2,0,1:T(8,128)S(1)} all-to-all(f32[8,16,640]{2,0,1:T(8,128)S(1)} %pad_maximum_fusion.3), channel_id=1, replica_groups=mesh['row'=8,'col'=16] {'col'}, dimensions={1} | all-to-all | bytes 655360 | tf_op jit(solution)/shard_map/all_to_all | solution.py:47
  163.3 6.3 %all-to-all-start.4 = ((f32[8,1,128]{2,1,0:T(1,128)}), f32[8,1,128]{2,1,0:T(1,128)S(1)}, u32[]{:S(2)}, u32[]{:S(2)}) async-start(f32[8,1,128]{2,1,0:T(1,128)} %broadcast_in_dim.19), calls=%async_computation.5 | async-start | bytes 8192 | tf_op jit(solution)/shard_map/all_to_all | solution.py:25
  169.6 6.4 %all-to-all-done.4 = f32[8,1,128]{2,1,0:T(1,128)S(1)} async-done(((f32[8,1,128]{2,1,0:T(1,128)}), f32[8,1,128]{2,1,0:T(1,128)S(1)}, u32[]{:S(2)}, u32[]{:S(2)}) %all-to-all-start.4) | async-done | bytes 4128 | tf_op jit(solution)/shard_map/all_to_all | solution.py:25
  176.1 1.1 broadcast_in_dim.17
  177.1 3.6 %all-to-all-start.3 = ((bf16[8,128,512]{2,1,0:T(8,128)(2,1)}), bf16[8,128,512]{2,1,0:T(8,128)(2,1)S(1)}, u32[]{:S(2)}, u32[]{:S(2)}) async-start(bf16[8,128,512]{2,1,0:T(8,128)(2,1)} %broadcast_in_dim.17), calls=%async_computation.4 | async-start | bytes 2097152 | tf_op jit(solution)/shard_map/all_to_all | solution.py:25
  180.9 0.7 slice.77
  181.8 16.7 %all-to-all-done.3 = bf16[8,128,512]{2,1,0:T(8,128)(2,1)S(1)} async-done(((bf16[8,128,512]{2,1,0:T(8,128)(2,1)}), bf16[8,128,512]{2,1,0:T(8,128)(2,1)S(1)}, u32[]{:S(2)}, u32[]{:S(2)}) %all-to-all-start.3) | async-done | bytes 1048608 | tf_op jit(solution)/shard_map/all_to_all | solution.py:25
  198.5 1.3 fusion.2
  199.7 10.2 %all-gather.7.cloned.1.call-done = bf16[1024,3584]{1,0:T(8,128)(2,1)} async-done(((bf16[64,3584]{1,0:T(8,128)(2,1)}), bf16[1024,3584]{1,0:T(8,128)(2,1)}) %all-gather.7.cloned.1.call-update) | async-done | bytes 7340048 | tf_op jit(solution)/shard_map/all_gather | solution.py:67
  209.9 9.3 %fusion.16 = bf16[512,3584]{1,0:T(8,128)(2,1)} fusion(bf16[1024,512]{1,0:T(8,128)(2,1)} %fusion.2, bf16[1024,3584]{1,0:T(8,128)(2,1)} %all-gather.7.cloned.1.call-done), kind=kOutput, calls=%fused_computation.41 | convolution fusion | flops 3758096384 | bytes 12058624 | tf_op jit(solution)/shard_map/td,tf->df/dot_general | solution.py:69
  219.1 39.1 %all-gather.9.cloned.1.call-done = bf16[1024,3584]{1,0:T(8,128)(2,1)} async-done(((bf16[64,3584]{1,0:T(8,128)(2,1)}), bf16[1024,3584]{1,0:T(8,128)(2,1)}) %all-gather.9.cloned.1.call-update) | async-done | bytes 7340048 | tf_op jit(solution)/shard_map/all_gather | solution.py:68
  258.2 7.5 %fusion.15 = f32[1024,512]{1,0:T(8,128)S(1)} fusion(bf16[1024,3584]{1,0:T(8,128)(2,1)} %all-gather.7.cloned.1.call-done, bf16[512,3584]{1,0:T(8,128)(2,1)} %param.17), kind=kOutput, calls=%fused_computation.40 | convolution fusion | flops 3758096384 | bytes 13107200 | tf_op jit(solution)/shard_map/tf,df->td/dot_general | solution.py:73
  265.8 5.1 %fusion.12 = (bf16[1024,512]{1,0:T(8,128)(2,1)}, f32[512]{0:T(512)S(1)}) fusion(f32[1024]{0:T(1024)S(1)} %bitcast.52, bf16[8,128,512]{2,1,0:T(8,128)(2,1)S(1)} %all-to-all-done.3, f32[1024,512]{1,0:T(8,128)S(1)} %fusion.15, bf16[1024,3584]{1,0:T(8,128)(2,1)S(1)} %copy-done.7, bf16[512,3584]{1,0:T(8,128)(2,1)S(1)} %copy-done.8), kind=kOutput, calls=%fused_computation.37 | convolution fusion | flops 3761241600 | bytes 15210496 | tf_op jit(solution)/shard_map/tf,df->td/dot_general | solution.py:74
  271.0 1.4 pad_maximum_fusion.1
  272.4 25.1 %all_to_all.59 = bf16[8,136,512]{2,1,0:T(8,128)(2,1)S(1)} all-to-all(bf16[8,136,512]{2,1,0:T(8,128)(2,1)S(1)} %pad_maximum_fusion.1), channel_id=1, replica_groups=mesh['row'=8,'col'=16] {'row'}, dimensions={0} | all-to-all | bytes 2228224 | tf_op jit(solution)/shard_map/all_to_all | solution.py:85
  297.8 0.9 pad_maximum_fusion.2
  298.6 5.4 %all-to-all-start.6 = ((f32[16,9,512]{2,1,0:T(8,128)}), f32[16,9,512]{2,1,0:T(8,128)S(1)}, u32[]{:S(2)}, u32[]{:S(2)}) async-start(f32[16,9,512]{2,1,0:T(8,128)} %pad_maximum_fusion.2), calls=%async_computation.7 | async-start | bytes 1048576 | tf_op jit(solution)/shard_map/all_to_all | solution.py:94
  304.0 8.7 %convolution_convert_fusion = bf16[512,3584]{1,0:T(8,128)(2,1)} fusion(bf16[1024,512]{1,0:T(8,128)(2,1)S(1)} %copy-done.3, bf16[1024,3584]{1,0:T(8,128)(2,1)} %all-gather.9.cloned.1.call-done), kind=kOutput, calls=%fused_computation | convolution fusion | flops 3759931392 | bytes 12058624 | tf_op jit(solution)/shard_map/td,tf->df/dot_general | solution.py:97
  312.7 1.6 all-to-all-done.6
  314.3 0.6 slice.84
  315.2 0.8 add_convert_fusion
  316.0 5.7 %convolution_convert_fusion.1 = bf16[2560,512]{1,0:T(8,128)(2,1)S(1)} fusion(bf16[1024,2560]{1,0:T(8,128)(2,1)} %all-gather.11.cloned.1.call-done, bf16[1024,512]{1,0:T(8,128)(2,1)} %bitcast.44), kind=kOutput, calls=%fused_computation.1 | convolution fusion | flops 2685665280 | bytes 8912896 | tf_op jit(solution)/shard_map/tf,td->fd/dot_general | solution.py:98
  321.7 2.1 pad_maximum_fusion
  (51 shorter events, 2.8 us)
Async XLA Ops:
  7.2 49.6 %all-gather.5.cloned.1.call-start = ((), (), s32[]{:S(2)}) async-start(), calls=%async_computation.8 | async-start | bytes 2228224 | tf_op jit(solution)/shard_map/all_gather | solution.py:54
  9.3 135.6 %reduce-scatter.2.cloned.1.call-start = ((), (), s32[]{:S(2)}) async-start(), calls=%async_computation.9 | async-start | bytes 15597568 | tf_op jit(solution)/shard_map/reduce_scatter | solution.py:59
  46.4 1.0 copy-start.4
  56.8 88.2 %copy-start.1 = (bf16[64,3584]{1,0:T(8,128)(2,1)S(1)}, bf16[64,3584]{1,0:T(8,128)(2,1)}, u32[]{:S(2)}) copy-start(bf16[64,3584]{1,0:T(8,128)(2,1)} %param.16) | copy-start | bytes 1376260
  56.8 88.1 %copy-start.2 = (bf16[64,3584]{1,0:T(8,128)(2,1)S(1)}, bf16[64,3584]{1,0:T(8,128)(2,1)}, u32[]{:S(2)}) copy-start(bf16[64,3584]{1,0:T(8,128)(2,1)} %param.15) | copy-start | bytes 1376260
  56.8 153.1 %all-gather.7.cloned.1.call-start = ((), (), s32[]{:S(2)}) async-start(), calls=%async_computation.10 | async-start | bytes 7798784 | tf_op jit(solution)/shard_map/all_gather | solution.py:67
  60.1 88.0 %copy-start = (bf16[8,8192]{1,0:T(8,128)(2,1)S(1)}, bf16[8,8192]{1,0:T(8,128)(2,1)}, u32[]{:S(2)}) copy-start(bf16[8,8192]{1,0:T(8,128)(2,1)} %param.12) | copy-start | bytes 393220
  147.5 34.2 %copy-start.6 = (f32[8192]{0:T(1024)S(1)}, f32[8192]{0:T(1024)}, u32[]{:S(2)}) copy-start(f32[8192]{0:T(1024)} %param.13) | copy-start | bytes 98308
  147.5 110.7 %all-gather.9.cloned.1.call-start = ((), (), s32[]{:S(2)}) async-start(), calls=%async_computation.11 | async-start | bytes 7798784 | tf_op jit(solution)/shard_map/all_gather | solution.py:68
  163.3 12.8 %all-to-all-start.4 = ((f32[8,1,128]{2,1,0:T(1,128)}), f32[8,1,128]{2,1,0:T(1,128)S(1)}, u32[]{:S(2)}, u32[]{:S(2)}) async-start(f32[8,1,128]{2,1,0:T(1,128)} %broadcast_in_dim.19), calls=%async_computation.5 | async-start | bytes 8192 | tf_op jit(solution)/shard_map/all_to_all | solution.py:25
  177.1 21.3 %all-to-all-start.3 = ((bf16[8,128,512]{2,1,0:T(8,128)(2,1)}), bf16[8,128,512]{2,1,0:T(8,128)(2,1)S(1)}, u32[]{:S(2)}, u32[]{:S(2)}) async-start(bf16[8,128,512]{2,1,0:T(8,128)(2,1)} %broadcast_in_dim.17), calls=%async_computation.4 | async-start | bytes 2097152 | tf_op jit(solution)/shard_map/all_to_all | solution.py:25
  180.7 135.2 %all-gather.11.cloned.1.call-start = ((), (), s32[]{:S(2)}) async-start(), calls=%async_computation.12 | async-start | bytes 5570560 | tf_op jit(solution)/shard_map/all_gather | solution.py:72
  258.2 7.5 %copy-start.7 = (bf16[1024,3584]{1,0:T(8,128)(2,1)S(1)}, bf16[1024,3584]{1,0:T(8,128)(2,1)}, u32[]{:S(2)}) copy-start(bf16[1024,3584]{1,0:T(8,128)(2,1)} %all-gather.9.cloned.1.call-done) | copy-start | bytes 22020100
  258.2 7.5 %copy-start.8 = (bf16[512,3584]{1,0:T(8,128)(2,1)S(1)}, bf16[512,3584]{1,0:T(8,128)(2,1)}, u32[]{:S(2)}) copy-start(bf16[512,3584]{1,0:T(8,128)(2,1)} %param.18) | copy-start | bytes 11010052
  271.0 33.0 %copy-start.3 = (bf16[1024,512]{1,0:T(8,128)(2,1)S(1)}, bf16[1024,512]{1,0:T(8,128)(2,1)}, u32[]{:S(2)}) copy-start(bf16[1024,512]{1,0:T(8,128)(2,1)} %fusion.2) | copy-start | bytes 3145732
  298.6 15.6 %all-to-all-start.6 = ((f32[16,9,512]{2,1,0:T(8,128)}), f32[16,9,512]{2,1,0:T(8,128)S(1)}, u32[]{:S(2)}, u32[]{:S(2)}) async-start(f32[16,9,512]{2,1,0:T(8,128)} %pad_maximum_fusion.2), calls=%async_computation.7 | async-start | bytes 1048576 | tf_op jit(solution)/shard_map/all_to_all | solution.py:94
  304.0 11.2 %copy-start.5 = (bf16[8,8192]{1,0:T(8,128)(2,1)S(1)}, bf16[8,8192]{1,0:T(8,128)(2,1)}, u32[]{:S(2)}) copy-start(bf16[8,8192]{1,0:T(8,128)(2,1)} %param.14) | copy-start | bytes 393220
Sparse Core Ops, SparseCore 0:
  10.2 45.7 all-gather.4
  58.4 86.4 reduce-scatter.1
  147.7 62.1 all-gather.6
  211.4 46.7 all-gather.8
  259.8 56.1 all-gather.10
where the time goes:
time: 331 us; the launch traced here: 330 us
  waiting for transfers between devices  159 us (48%)
  blocking collectives  76.2 us (23%)
  matrix products  48.8 us (15%)
  starting transfers between devices  15.6 us (5%)
  between operations  14 us (4%)
  other arithmetic  11 us (3%)
  local copies, waits for them, and re-layouts  5.29 us (2%)
    reduce_scatter x1, waiting for transfers between devices, local(): lax.psum_scatter(partial_grad, 'col', scatter_dimension=0, tiled=True)  84.9 us
    all_gather x1, waiting for transfers between devices, local(): up_piece = lax.all_gather(up_block, 'col', axis=0, tiled=True)  39.1 us
    all_to_all x1, blocking collectives, local(): got = lax.all_to_all(sent, 'row', split_axis=0, concat_axis=0, tiled=True)  25.1 us
    all_to_all x1, blocking collectives, row_gather(): got = lax.all_to_all(copies, 'row', split_axis=0, concat_axis=0, tiled=True)  23.5 us
    all_to_all x2, waiting for transfers between devices, row_gather(): got = lax.all_to_all(copies, 'row', split_axis=0, concat_axis=0, tiled=True)  23.1 us
    all_to_all x1, blocking collectives, local(): lax.all_to_all(packed, 'col', split_axis=1, concat_axis=0, tiled=True)  14.1 us
    all_to_all x1, blocking collectives, local(): lax.all_to_all(grad_out, 'col', split_axis=1, concat_axis=0, tiled=True)  13.4 us
    all_gather x1, waiting for transfers between devices, local(): gate_piece = lax.all_gather(gate_block, 'col', axis=0, tiled=True)  10.2 us
  transfers between devices with their start and end apart: 8, of which 6 were waited for; matrix products, arithmetic and copies ran while one was open for 16% of the time, Pallas kernels for 0%

commit v1 on v0

--- a/solution.py
+++ b/solution.py
@@ -36,7 +36,9 @@
     gain_tile = lax.dynamic_slice_in_dim(gain, lax.axis_index("col") * tile, tile)
     mine_rows = tokens.shape[0]
     lanes = 128
-    grid_grad = lax.all_to_all(grad_out, "col", split_axis=1, concat_axis=0, tiled=True)
+    pieces = jnp.split(grad_out, lax.axis_size("col"), axis=1)
+    received = lax.all_to_all(jnp.stack(pieces), "col", 0, 0)
+    grid_grad = jnp.concatenate(received, axis=0)
     packed = jnp.concatenate(
         [
             tokens_wide.reshape(mine_rows, cols, tile),

time: 331 us -> 337 us (1.018)
  local copies, waits for them, and re-layouts: 5.29 us -> 16.8 us
  waiting for transfers between devices: 159 us -> 154 us
    unnamed x18 -> x35, local copies, waits for them, and re-layouts: 1.05 us -> 11.9 us
    reduce_scatter x1, waiting for transfers between devices: 84.9 us -> 79.3 us  [local(): lax.psum_scatter(partial_grad, 'col', scatter_dimension=0, tiled=True)]
  transfers between devices with their start and end apart: 8 -> 8, of which waited for: 6 -> 6; matrix products, arithmetic and copies ran while one was open for 16% -> 18% of each run, Pallas kernels for 0% -> 0%
where the time goes in v1:
time: 337 us; the launch traced here: 335 us
  waiting for transfers between devices  154 us (46%)
  blocking collectives  77.6 us (23%)
  matrix products  46.7 us (14%)
  local copies, waits for them, and re-layouts  16.8 us (5%)
  starting transfers between devices  15.3 us (5%)
  between operations  14 us (4%)
  other arithmetic  11 us (3%)
    reduce_scatter x1, waiting for transfers between devices, local(): lax.psum_scatter(partial_grad, 'col', scatter_dimension=0, tiled=True)  79.3 us
    all_gather x1, waiting for transfers between devices, local(): up_piece = lax.all_gather(up_block, 'col', axis=0, tiled=True)  38.9 us
    all_to_all x1, blocking collectives, local(): got = lax.all_to_all(sent, 'row', split_axis=0, concat_axis=0, tiled=True)  25.1 us
    all_to_all x1, blocking collectives, row_gather(): got = lax.all_to_all(copies, 'row', split_axis=0, concat_axis=0, tiled=True)  24.3 us
    all_to_all x2, waiting for transfers between devices, row_gather(): got = lax.all_to_all(copies, 'row', split_axis=0, concat_axis=0, tiled=True)  23.1 us
    all_to_all x1, blocking collectives, local(): lax.all_to_all(packed, 'col', split_axis=1, concat_axis=0, tiled=True)  14.3 us
    all_to_all x1, blocking collectives, local(): received = lax.all_to_all(jnp.stack(pieces), 'col', 0, 0)  13.9 us
    unnamed x35, local copies, waits for them, and re-layouts  11.9 us
  transfers between devices with their start and end apart: 8, of which 6 were waited for; matrix products, arithmetic and copies ran while one was open for 18% of the time, Pallas kernels for 0%

profile of v1, /device:TPU:1, one launch (start us, length us, event | category | flops | bytes accessed | tf_op | source)
XLA Modules:
  0.0 335.3 jit_solution(6340046844845479934)
XLA Ops:
  7.2 1.4 fusion.4
  9.4 0.9 constant_dynamic-update-slice_fusion.15
  10.3 0.9 constant_dynamic-update-slice_fusion.14
  20.9 13.9 %all_to_all.45 = bf16[16,8,512]{2,1,0:T(8,128)(2,1)S(1)} all-to-all(bf16[16,8,512]{2,1,0:T(8,128)(2,1)S(1)} %constant_dynamic-update-slice_fusion), channel_id=1, replica_groups=mesh['row'=8,'col'=16] {'col'}, dimensions={0} | all-to-all | bytes 262144 | tf_op jit(solution)/shard_map/all_to_all | solution.py:40
  34.9 24.3 %all_to_all.46 = bf16[8,128,512]{2,1,0:T(8,128)(2,1)S(1)} all-to-all(bf16[8,128,512]{2,1,0:T(8,128)(2,1)S(1)} %broadcast_in_dim.15), channel_id=1, replica_groups=mesh['row'=8,'col'=16] {'row'}, dimensions={0} | all-to-all | bytes 2097152 | tf_op jit(solution)/shard_map/all_to_all | solution.py:25
  59.2 1.0 copy-done.4
  60.2 7.3 %fusion.13 = f32[1024,3584]{1,0:T(8,128)} fusion(bf16[1024,512]{1,0:T(8,128)(2,1)S(1)} %bitcast.71, bf16[3584,512]{1,0:T(8,128)(2,1)S(1)} %copy-done.8), kind=kOutput, calls=%fused_computation.54 | convolution fusion | flops 3758096384 | bytes 19398656 | tf_op jit(solution)/shard_map/td,fd->tf/dot_general | solution.py:57
  67.7 3.2 fusion.14
  70.9 79.3 %reduce-scatter.2.cloned.1.call-done = f32[64,3584]{1,0:T(8,128)} async-done(((f32[1024,3584]{1,0:T(8,128)}), f32[64,3584]{1,0:T(8,128)}) %reduce-scatter.2.cloned.1.call-update) | async-done | bytes 917520 | tf_op jit(solution)/shard_map/reduce_scatter | solution.py:61
  150.1 2.5 multiply_convert_fusion
  153.6 14.3 %all_to_all.47 = f32[8,16,640]{2,0,1:T(8,128)S(1)} all-to-all(f32[8,16,640]{2,0,1:T(8,128)S(1)} %pad_maximum_fusion.3), channel_id=1, replica_groups=mesh['row'=8,'col'=16] {'col'}, dimensions={1} | all-to-all | bytes 655360 | tf_op jit(solution)/shard_map/all_to_all | solution.py:49
  168.6 5.9 %all-to-all-start.4 = ((f32[8,1,128]{2,1,0:T(1,128)}), f32[8,1,128]{2,1,0:T(1,128)S(1)}, u32[]{:S(2)}, u32[]{:S(2)}) async-start(f32[8,1,128]{2,1,0:T(1,128)} %broadcast_in_dim.19), calls=%async_computation.5 | async-start | bytes 8192 | tf_op jit(solution)/shard_map/all_to_all | solution.py:25
  174.6 6.4 %all-to-all-done.4 = f32[8,1,128]{2,1,0:T(1,128)S(1)} async-done(((f32[8,1,128]{2,1,0:T(1,128)}), f32[8,1,128]{2,1,0:T(1,128)S(1)}, u32[]{:S(2)}, u32[]{:S(2)}) %all-to-all-start.4) | async-done | bytes 4128 | tf_op jit(solution)/shard_map/all_to_all | solution.py:25
  181.0 1.1 broadcast_in_dim.17
  182.1 3.6 %all-to-all-start.3 = ((bf16[8,128,512]{2,1,0:T(8,128)(2,1)}), bf16[8,128,512]{2,1,0:T(8,128)(2,1)S(1)}, u32[]{:S(2)}, u32[]{:S(2)}) async-start(bf16[8,128,512]{2,1,0:T(8,128)(2,1)} %broadcast_in_dim.17), calls=%async_computation.4 | async-start | bytes 2097152 | tf_op jit(solution)/shard_map/all_to_all | solution.py:25
  185.9 0.8 slice.77
  186.7 16.7 %all-to-all-done.3 = bf16[8,128,512]{2,1,0:T(8,128)(2,1)S(1)} async-done(((bf16[8,128,512]{2,1,0:T(8,128)(2,1)}), bf16[8,128,512]{2,1,0:T(8,128)(2,1)S(1)}, u32[]{:S(2)}, u32[]{:S(2)}) %all-to-all-start.3) | async-done | bytes 1048608 | tf_op jit(solution)/shard_map/all_to_all | solution.py:25
  203.4 1.3 fusion.2
  204.7 10.4 %all-gather.7.cloned.1.call-done = bf16[1024,3584]{1,0:T(8,128)(2,1)} async-done(((bf16[64,3584]{1,0:T(8,128)(2,1)}), bf16[1024,3584]{1,0:T(8,128)(2,1)}) %all-gather.7.cloned.1.call-update) | async-done | bytes 7340048 | tf_op jit(solution)/shard_map/all_gather | solution.py:69
  215.1 9.3 %fusion.16 = bf16[512,3584]{1,0:T(8,128)(2,1)} fusion(bf16[1024,512]{1,0:T(8,128)(2,1)} %fusion.2, bf16[1024,3584]{1,0:T(8,128)(2,1)} %all-gather.7.cloned.1.call-done), kind=kOutput, calls=%fused_computation.57 | convolution fusion | flops 3758096384 | bytes 12058624 | tf_op jit(solution)/shard_map/td,tf->df/dot_general | solution.py:71
  224.3 38.9 %all-gather.9.cloned.1.call-done = bf16[1024,3584]{1,0:T(8,128)(2,1)} async-done(((bf16[64,3584]{1,0:T(8,128)(2,1)}), bf16[1024,3584]{1,0:T(8,128)(2,1)}) %all-gather.9.cloned.1.call-update) | async-done | bytes 7340048 | tf_op jit(solution)/shard_map/all_gather | solution.py:70
  263.3 7.5 %fusion.15 = f32[1024,512]{1,0:T(8,128)S(1)} fusion(bf16[1024,3584]{1,0:T(8,128)(2,1)} %all-gather.7.cloned.1.call-done, bf16[512,3584]{1,0:T(8,128)(2,1)} %param.17), kind=kOutput, calls=%fused_computation.56 | convolution fusion | flops 3758096384 | bytes 13107200 | tf_op jit(solution)/shard_map/tf,df->td/dot_general | solution.py:75
  270.8 5.1 %fusion.12 = (bf16[1024,512]{1,0:T(8,128)(2,1)}, f32[512]{0:T(512)S(1)}) fusion(f32[1024]{0:T(1024)S(1)} %bitcast.80, bf16[8,128,512]{2,1,0:T(8,128)(2,1)S(1)} %all-to-all-done.3, f32[1024,512]{1,0:T(8,128)S(1)} %fusion.15, bf16[1024,3584]{1,0:T(8,128)(2,1)S(1)} %copy-done.7, bf16[512,3584]{1,0:T(8,128)(2,1)S(1)} %copy-done.9), kind=kOutput, calls=%fused_computation.53 | convolution fusion | flops 3761241600 | bytes 15210496 | tf_op jit(solution)/shard_map/tf,df->td/dot_general | solution.py:76
  276.0 1.4 pad_maximum_fusion.1
  277.4 25.1 %all_to_all.48 = bf16[8,136,512]{2,1,0:T(8,128)(2,1)S(1)} all-to-all(bf16[8,136,512]{2,1,0:T(8,128)(2,1)S(1)} %pad_maximum_fusion.1), channel_id=1, replica_groups=mesh['row'=8,'col'=16] {'row'}, dimensions={0} | all-to-all | bytes 2228224 | tf_op jit(solution)/shard_map/all_to_all | solution.py:87
  302.8 0.9 pad_maximum_fusion.2
  303.6 5.4 %all-to-all-start.6 = ((f32[16,9,512]{2,1,0:T(8,128)}), f32[16,9,512]{2,1,0:T(8,128)S(1)}, u32[]{:S(2)}, u32[]{:S(2)}) async-start(f32[16,9,512]{2,1,0:T(8,128)} %pad_maximum_fusion.2), calls=%async_computation.7 | async-start | bytes 1048576 | tf_op jit(solution)/shard_map/all_to_all | solution.py:96
  309.0 8.7 %convolution_convert_fusion = bf16[512,3584]{1,0:T(8,128)(2,1)} fusion(bf16[1024,512]{1,0:T(8,128)(2,1)S(1)} %copy-done.3, bf16[1024,3584]{1,0:T(8,128)(2,1)} %all-gather.9.cloned.1.call-done), kind=kOutput, calls=%fused_computation | convolution fusion | flops 3759931392 | bytes 12058624 | tf_op jit(solution)/shard_map/td,tf->df/dot_general | solution.py:99
  317.7 1.6 all-to-all-done.6
  320.2 0.8 add_convert_fusion
  321.0 5.7 %convolution_convert_fusion.1 = bf16[2560,512]{1,0:T(8,128)(2,1)S(1)} fusion(bf16[1024,2560]{1,0:T(8,128)(2,1)} %all-gather.11.cloned.1.call-done, bf16[1024,512]{1,0:T(8,128)(2,1)} %bitcast.73), kind=kOutput, calls=%fused_computation.1 | convolution fusion | flops 2685665280 | bytes 8912896 | tf_op jit(solution)/shard_map/tf,td->fd/dot_general | solution.py:100
  326.7 2.1 pad_maximum_fusion
  (69 shorter events, 13.9 us)
Async XLA Ops:
  7.2 60.4 %all-gather.5.cloned.1.call-start = ((), (), s32[]{:S(2)}) async-start(), calls=%async_computation.8 | async-start | bytes 2228224 | tf_op jit(solution)/shard_map/all_gather | solution.py:56
  9.3 140.8 %reduce-scatter.2.cloned.1.call-start = ((), (), s32[]{:S(2)}) async-start(), calls=%async_computation.9 | async-start | bytes 15597568 | tf_op jit(solution)/shard_map/reduce_scatter | solution.py:61
  9.4 50.9 %copy-start.8 = (bf16[3584,512]{1,0:T(8,128)(2,1)S(1)}, bf16[3584,512]{1,0:T(8,128)(2,1)}, u32[]{:S(2)}) copy-start(bf16[3584,512]{1,0:T(8,128)(2,1)} %param.19) | copy-start | bytes 11010052
  59.2 1.0 copy-start.4
  67.6 82.6 %copy-start.1 = (bf16[64,3584]{1,0:T(8,128)(2,1)S(1)}, bf16[64,3584]{1,0:T(8,128)(2,1)}, u32[]{:S(2)}) copy-start(bf16[64,3584]{1,0:T(8,128)(2,1)} %param.16) | copy-start | bytes 1376260
  67.6 82.5 %copy-start.2 = (bf16[64,3584]{1,0:T(8,128)(2,1)S(1)}, bf16[64,3584]{1,0:T(8,128)(2,1)}, u32[]{:S(2)}) copy-start(bf16[64,3584]{1,0:T(8,128)(2,1)} %param.15) | copy-start | bytes 1376260
  67.6 147.5 %all-gather.7.cloned.1.call-start = ((), (), s32[]{:S(2)}) async-start(), calls=%async_computation.10 | async-start | bytes 7798784 | tf_op jit(solution)/shard_map/all_gather | solution.py:69
  70.9 82.4 %copy-start = (bf16[8,8192]{1,0:T(8,128)(2,1)S(1)}, bf16[8,8192]{1,0:T(8,128)(2,1)}, u32[]{:S(2)}) copy-start(bf16[8,8192]{1,0:T(8,128)(2,1)} %param.12) | copy-start | bytes 393220
  152.7 34.0 %copy-start.6 = (f32[8192]{0:T(1024)S(1)}, f32[8192]{0:T(1024)}, u32[]{:S(2)}) copy-start(f32[8192]{0:T(1024)} %param.13) | copy-start | bytes 98308
  152.7 110.5 %all-gather.9.cloned.1.call-start = ((), (), s32[]{:S(2)}) async-start(), calls=%async_computation.11 | async-start | bytes 7798784 | tf_op jit(solution)/shard_map/all_gather | solution.py:70
  168.6 12.4 %all-to-all-start.4 = ((f32[8,1,128]{2,1,0:T(1,128)}), f32[8,1,128]{2,1,0:T(1,128)S(1)}, u32[]{:S(2)}, u32[]{:S(2)}) async-start(f32[8,1,128]{2,1,0:T(1,128)} %broadcast_in_dim.19), calls=%async_computation.5 | async-start | bytes 8192 | tf_op jit(solution)/shard_map/all_to_all | solution.py:25
  182.1 21.3 %all-to-all-start.3 = ((bf16[8,128,512]{2,1,0:T(8,128)(2,1)}), bf16[8,128,512]{2,1,0:T(8,128)(2,1)S(1)}, u32[]{:S(2)}, u32[]{:S(2)}) async-start(bf16[8,128,512]{2,1,0:T(8,128)(2,1)} %broadcast_in_dim.17), calls=%async_computation.4 | async-start | bytes 2097152 | tf_op jit(solution)/shard_map/all_to_all | solution.py:25
  185.7 135.3 %all-gather.11.cloned.1.call-start = ((), (), s32[]{:S(2)}) async-start(), calls=%async_computation.12 | async-start | bytes 5570560 | tf_op jit(solution)/shard_map/all_gather | solution.py:74
  263.2 7.5 %copy-start.7 = (bf16[1024,3584]{1,0:T(8,128)(2,1)S(1)}, bf16[1024,3584]{1,0:T(8,128)(2,1)}, u32[]{:S(2)}) copy-start(bf16[1024,3584]{1,0:T(8,128)(2,1)} %all-gather.9.cloned.1.call-done) | copy-start | bytes 22020100
  263.3 7.5 %copy-start.9 = (bf16[512,3584]{1,0:T(8,128)(2,1)S(1)}, bf16[512,3584]{1,0:T(8,128)(2,1)}, u32[]{:S(2)}) copy-start(bf16[512,3584]{1,0:T(8,128)(2,1)} %param.18) | copy-start | bytes 11010052
  276.0 33.0 %copy-start.3 = (bf16[1024,512]{1,0:T(8,128)(2,1)S(1)}, bf16[1024,512]{1,0:T(8,128)(2,1)}, u32[]{:S(2)}) copy-start(bf16[1024,512]{1,0:T(8,128)(2,1)} %fusion.2) | copy-start | bytes 3145732
  303.6 15.6 %all-to-all-start.6 = ((f32[16,9,512]{2,1,0:T(8,128)}), f32[16,9,512]{2,1,0:T(8,128)S(1)}, u32[]{:S(2)}, u32[]{:S(2)}) async-start(f32[16,9,512]{2,1,0:T(8,128)} %pad_maximum_fusion.2), calls=%async_computation.7 | async-start | bytes 1048576 | tf_op jit(solution)/shard_map/all_to_all | solution.py:96
  309.0 11.2 %copy-start.5 = (bf16[8,8192]{1,0:T(8,128)(2,1)S(1)}, bf16[8,8192]{1,0:T(8,128)(2,1)}, u32[]{:S(2)}) copy-start(bf16[8,8192]{1,0:T(8,128)(2,1)} %param.14) | copy-start | bytes 393220
Sparse Core Ops, SparseCore 0:
  10.2 40.1 all-gather.4
  67.7 82.3 reduce-scatter.1
  152.8 62.2 all-gather.6
  216.6 46.5 all-gather.8
  264.8 56.1 all-gather.10
